TPU v7x, 512 devices: a whole 4x8x8 slice. The times are simulated.
512 devices in a mesh: req: 4 (over x), exp: 8 (over z), shard: 16 (over y, core).
Axes of the slice: x: 4, y: 8, z: 8, core: 2. Of those that a mesh axis runs over, the one named last changes fastest.
Arguments:
- query_stretch: bfloat16 [8, 128, 2304], P('req', 'exp'), may hold values from -8 to 8
- resid_stretch: bfloat16 [8, 128, 2304], P('req', 'exp'), may hold values from -30 to 30
- route_ids: int32 [8, 128, 2], P('req', 'exp'), may hold values from 0 to 7, all different within a row; in each aligned block of 16 rows (0 to 15, 16 to 31, ..., all dimensions but the last counted through in order) at most 6 rows name the same one
- route_probs: bfloat16 [8, 128, 2], P('req', 'exp'), may hold values from 0.19921875 to 1
- request_order: int32 [8], replicated, may hold values from 0 to 7, each once
- prior_pages: int32 [4, 2], P('req'), may hold values from 63 to 189, as said below
- page_order: int32 [4, 256], P('req'), may hold values from 0 to 255, each once within a row
- key_pool: bfloat16 [4, 256, 64, 2304], P('req', ('exp', 'shard')), may hold values from -8 to 8
- value_pool: bfloat16 [4, 256, 64, 2304], P('req', ('exp', 'shard')), may hold values from -6 to 6
- norm_gain: float32 [2304], replicated, may hold values from 0.4 to 2.5
- out_proj: bfloat16 [2304, 2304], P('shard'), may hold values from -0.125 to 0.125
- gate_up: bfloat16 [8, 2, 2880, 2304], P('exp', None, 'shard'), may hold values from -0.125 to 0.125
- down_proj: bfloat16 [8, 2880, 2304], P('exp', 'shard'), may hold values from -0.109375 to 0.109375
Outputs:
- mixed_out: bfloat16 [8, 128, 2304], P('req', 'exp')
Inputs may be any that keep to these rules, and one draw needn't show every extreme that they name: `route_ids`: each row names 2 different experts. In each aligned block of 16 rows (one request's tokens b * 16 to (b + 1) * 16 - 1) no expert is named by more than 6 rows, a bound that some block reaches. `request_order`: A permutation of the requests. `prior_pages`: in each group the 2 counts sum to 252, so that the pool is full; one member of every group has exactly 189. `page_order`: each row is a permutation of the group's pool pages.
All inputs are finite; a program needn't handle non-finite values.
Results may differ from a plain program's by a relative error of at most 0.02.
Values may be sent and summed in bfloat16 or wider, within the bound.
No kernel may reach another device: no remote copies, remote signals or barrier semaphores. Data moves between devices by JAX's collectives and lax.ppermute only.
A program may use at most 64 MiB of HBM per device.

v0:
```python
import math
import jax
import jax.numpy as jnp
from jax import lax
from jax.sharding import PartitionSpec as P

H = 36
NEG_FILL = -1e30
EPSILON = 1e-06


def expert_rows(received, gate_up, down_proj):
    width = received.shape[-1]
    flat_rows = received.reshape(-1, width)
    both = lax.dot_general(
        flat_rows, gate_up[0], (((1,), (2,)), ((), ())), preferred_element_type=jnp.float32
    )
    active = (jax.nn.silu(both[:, 0]) * both[:, 1]).astype(jnp.bfloat16)
    partial_out = jnp.dot(active, down_proj[0], preferred_element_type=jnp.float32)
    return partial_out.reshape(received.shape)


def on_device(
    query_stretch,
    resid_stretch,
    route_ids,
    route_probs,
    request_order,
    prior_pages,
    page_order,
    key_pool,
    value_pool,
    norm_gain,
    out_proj,
    gate_up,
    down_proj,
):
    members = prior_pages.shape[1]
    tokens_here = query_stretch.shape[1]
    width = query_stretch.shape[2]
    head_size = width // H
    group_index = lax.axis_index("req")
    exp_index = lax.axis_index("exp")
    shard_index = lax.axis_index("shard")
    shard_count = lax.axis_size("shard")
    experts_count = lax.axis_size("exp")
    all_query, all_resid, all_ids, all_probs = (
        lax.all_gather(query_stretch, "req", axis=0, tiled=True),
        lax.all_gather(resid_stretch, "req", axis=0, tiled=True),
        lax.all_gather(route_ids, "req", axis=0, tiled=True),
        lax.all_gather(route_probs, "req", axis=0, tiled=True),
    )
    served = lax.dynamic_slice_in_dim(request_order, group_index * members, members)
    served_query = jnp.take(all_query, served, axis=0)
    served_resid = jnp.take(all_resid, served, axis=0)
    served_ids = jnp.take(all_ids, served, axis=0)
    served_probs = jnp.take(all_probs, served, axis=0)
    group_query = lax.all_gather(served_query, "exp", axis=1, tiled=True)
    stretch_len = group_query.shape[1]
    pages_here = key_pool.shape[1]
    page_size = key_pool.shape[2]
    device_index = exp_index * shard_count + shard_index
    physical = device_index * pages_here + jnp.arange(pages_here, dtype=jnp.int32)
    page_row = page_order[0]
    pool_size = page_row.shape[0]
    matched = page_row[None, :] == physical[:, None]
    located = jnp.sum(
        jnp.where(matched, jnp.arange(pool_size, dtype=jnp.int32)[None, :], 0), axis=1
    )
    prior_row = prior_pages[0]
    page_counts = prior_row + stretch_len // page_size
    page_ends = jnp.cumsum(page_counts)
    page_starts = page_ends - page_counts
    owner_slot = jnp.sum((located[:, None] >= page_ends[None, :]).astype(jnp.int32), axis=1)
    owner_hot = owner_slot[:, None] == jnp.arange(members, dtype=jnp.int32)[None, :]
    logical = located - jnp.sum(jnp.where(owner_hot, page_starts[None, :], 0), axis=1)
    prior_here = jnp.sum(jnp.where(owner_hot, prior_row[None, :], 0), axis=1)
    key_place = logical[:, None] * page_size + jnp.arange(page_size, dtype=jnp.int32)[None, :]
    query_place = (
        prior_here[:, None] * page_size + jnp.arange(stretch_len, dtype=jnp.int32)[None, :]
    )
    visible = key_place[:, None, :] <= query_place[:, :, None]
    page_query = jnp.take(group_query, owner_slot, axis=0).reshape(
        pages_here, stretch_len, H, head_size
    )
    key_rows = key_pool[0].reshape(pages_here, page_size, H, head_size)
    value_rows = value_pool[0].reshape(pages_here, page_size, H, head_size)
    scores = jnp.einsum(
        "pqhd,pkhd->phqk", page_query, key_rows, preferred_element_type=jnp.float32
    ) * (1.0 / math.sqrt(head_size))
    scores = jnp.where(visible[:, None, :, :], scores, NEG_FILL)
    page_peak = jnp.max(scores, axis=3)
    local_peak = jnp.max(
        jnp.where(owner_hot[:, :, None, None], page_peak[:, None], NEG_FILL), axis=0
    )
    row_peak = lax.pmax(local_peak, ("exp", "shard"))
    peak_here = jnp.take(row_peak, owner_slot, axis=0)
    weights_bf = jnp.where(
        visible[:, None, :, :], jnp.exp(scores - peak_here[..., None]), 0.0
    ).astype(jnp.bfloat16)
    page_totals = jnp.sum(weights_bf, axis=3, dtype=jnp.float32)
    page_context = jnp.einsum(
        "phqk,pkhd->pqhd", weights_bf, value_rows, preferred_element_type=jnp.float32
    )
    page_context = page_context.reshape(pages_here, stretch_len, width)
    context = jnp.sum(jnp.where(owner_hot[:, :, None, None], page_context[:, None], 0.0), axis=0)
    totals = jnp.sum(jnp.where(owner_hot[:, :, None, None], page_totals[:, None], 0.0), axis=0)
    context_all, totals_all = lax.psum((context, totals), ("exp", "shard"))
    context_mine = lax.dynamic_slice_in_dim(context_all, exp_index * tokens_here, tokens_here, 1)
    totals_mine = lax.dynamic_slice_in_dim(totals_all, exp_index * tokens_here, tokens_here, 2)
    per_head = context_mine.reshape(members, tokens_here, H, head_size)
    attended = (
        (per_head / jnp.transpose(totals_mine, (0, 2, 1))[..., None])
        .reshape(members, tokens_here, width)
        .astype(jnp.bfloat16)
    )
    projected_part = lax.dot_general(
        attended, out_proj, (((2,), (1,)), ((), ())), preferred_element_type=jnp.float32
    ).astype(jnp.bfloat16)
    projected = lax.all_gather(projected_part, "shard", axis=2, tiled=True)
    hidden_state = served_resid.astype(jnp.float32) + projected.astype(jnp.float32)
    mean_square = jnp.mean(hidden_state * hidden_state, axis=2, keepdims=True)
    normed = (hidden_state * lax.rsqrt(mean_square + EPSILON) * norm_gain).astype(jnp.bfloat16)
    top_count = served_ids.shape[2]
    capacity = min(tokens_here, max(2, 3 * tokens_here * top_count // (2 * experts_count)))
    flat_ids = served_ids.reshape(members, tokens_here * top_count)
    expert_hot = (
        flat_ids[:, :, None] == jnp.arange(experts_count, dtype=jnp.int32)[None, None, :]
    ).astype(jnp.int32)
    before = jnp.cumsum(expert_hot, axis=1) - expert_hot
    slot_place = jnp.sum(before * expert_hot, axis=2)
    slot_hot = (
        slot_place[:, :, None] == jnp.arange(capacity, dtype=jnp.int32)[None, None, :]
    ).astype(jnp.int32)
    place_table = (expert_hot[:, :, :, None] * slot_hot[:, :, None, :]).reshape(
        members, tokens_here, top_count, experts_count, capacity
    )
    pick_table = jnp.sum(place_table, axis=2).astype(jnp.bfloat16)
    sent_rows = jnp.einsum(
        "jtnc,jtd->njcd", pick_table, normed, preferred_element_type=jnp.float32
    ).astype(jnp.bfloat16)
    share_table = jnp.sum(
        place_table.astype(jnp.bfloat16) * served_probs[:, :, :, None, None], axis=2
    )
    partial_out = expert_rows(
        lax.all_to_all(sent_rows, "exp", split_axis=0, concat_axis=0, tiled=True),
        gate_up,
        down_proj,
    )
    expert_out = lax.psum(partial_out.astype(jnp.bfloat16), "shard")
    returned = lax.all_to_all(expert_out, "exp", split_axis=0, concat_axis=0, tiled=True)
    moe_term = jnp.einsum(
        "jtnc,njcd->jtd", share_table, returned, preferred_element_type=jnp.float32
    )
    mixed_out = (hidden_state + moe_term).astype(jnp.bfloat16)
    return mixed_out


def solution(mesh):
    return jax.shard_map(
        on_device,
        mesh=mesh,
        in_specs=(
            P("req", "exp", None),
            P("req", "exp", None),
            P("req", "exp", None),
            P("req", "exp", None),
            P(),
            P("req", None),
            P("req", None),
            P("req", ("exp", "shard"), None, None),
            P("req", ("exp", "shard"), None, None),
            P(),
            P("shard", None),
            P("exp", None, "shard", None),
            P("exp", "shard", None),
        ),
        out_specs=P("req", "exp", None),
        check_vma=False,
    )
```

profile of v0, /device:TPU:1, one launch (start us, length us, event | category | flops | bytes accessed | tf_op | source)
XLA Modules:
  0.0 1259.9 jit_solution(11993732823770950947)
XLA Ops:
  7.4 11.4 all_gather.19
  20.2 8.2 all_gather.22
  32.6 2.8 reshape_squeeze.6
  36.9 10.4 all_gather.18
  47.8 18.5 %all-gather.2.cloned.1.call-done = bf16[2,128,2304]{2,1,0:T(8,128)(2,1)} async-done(((bf16[2,16,2304]{2,1,0:T(8,128)(2,1)}), bf16[2,128,2304]{2,1,0:T(8,128)(2,1)}) %all-gather.2.cloned.1.call-update) | async-done | bytes 1179664 | tf_op jit(solution)/shard_map/all_gather | solution.py:58
  66.3 1.9 gather_fusion
  68.2 1.4 copy.90
  69.6 3.8 fusion.3
  73.6 490.0 %pmax.7 = f32[2,36,128]{2,1,0:T(8,128)S(1)} all-reduce(f32[2,36,128]{2,1,0:T(8,128)S(1)} %copy.92), channel_id=1, replica_groups=mesh['req'=4,'exp'=8,'shard'=16] {'exp','shard'}, use_global_device_ids=true, to_apply=%region_7.9 | all-reduce | flops 9216 | bytes 73728 | tf_op jit(solution)/shard_map/pmax | solution.py:96
  564.2 3.7 fusion.32
  567.9 3.1 copy.94
  571.0 3.7 select_reduce_fusion
  576.4 2.4 convert_reduce_fusion
  578.9 491.2 %psum.22 = f32[2,36,128]{2,0,1:T(2,128)S(1)} all-reduce(f32[2,36,128]{2,0,1:T(2,128)S(1)} %select_reduce_fusion.1), channel_id=1, replica_groups=mesh['req'=4,'exp'=8,'shard'=16] {'exp','shard'}, use_global_device_ids=true, to_apply=%region_12.14 | all-reduce | flops 9216 | bytes 73728 | tf_op jit(solution)/shard_map/psum | solution.py:108
  1070.8 1.5 convolution_convert_fusion.2
  1072.4 23.8 %all_gather.21 = bf16[2,16,2304]{1,0,2:T(2,128)(2,1)S(1)} all-gather(bf16[2,16,144]{1,0,2:T(2,128)(2,1)S(1)} %copy.96), channel_id=1, replica_groups=mesh['req'=4,'exp'=8,'shard'=16] {'shard'}, dimensions={2}, use_global_device_ids=true | all-gather | bytes 156672 | tf_op jit(solution)/shard_map/all_gather | solution.py:120
  1096.3 1.4 copy.97
  1098.6 20.1 %all_to_all.10 = bf16[8,2,6,2304]{3,1,2,0:T(2,128)(2,1)S(1)} all-to-all(bf16[8,2,6,2304]{3,1,2,0:T(2,128)(2,1)S(1)} %copy.100), channel_id=1, replica_groups=mesh['req'=4,'exp'=8,'shard'=16] {'exp'}, dimensions={0} | all-to-all | bytes 884736 | tf_op jit(solution)/shard_map/all_to_all | solution.py:146
  1119.6 1.6 fusion.4
  1122.5 105.0 %all-reduce.5.cloned.1.call-done = bf16[8,2,6,2304]{3,0,2,1:T(8,128)(2,1)} async-done(((bf16[8,2,6,2304]{3,0,2,1:T(8,128)(2,1)}), bf16[8,2,6,2304]{3,0,2,1:T(8,128)(2,1)}) %all-reduce.5.cloned.1.call-update) | async-done | bytes 442384 | tf_op jit(solution)/shard_map/psum | solution.py:150
  1227.5 2.1 copy.105
  1229.6 6.7 all-to-all-start.1
  1236.3 7.9 all_gather.23
  1244.9 7.6 all-to-all-done.1
  (83 shorter events, 16.3 us)
Async XLA Ops:
  6.5 1113.1 %copy-start = (bf16[1,2,180,2304]{3,1,2,0:T(2,128)(2,1)S(1)}, bf16[1,2,180,2304]{3,1,2,0:T(2,128)(2,1)}, u32[]{:S(2)}) copy-start(bf16[1,2,180,2304]{3,1,2,0:T(2,128)(2,1)} %param.26) | copy-start | bytes 4976644
  6.5 28.8 %copy-start.3 = (bf16[1,2,64,2304]{3,2,1,0:T(8,128)(2,1)S(1)}, bf16[1,2,64,2304]{3,2,1,0:T(8,128)(2,1)}, u32[]{:S(2)}) copy-start(bf16[1,2,64,2304]{3,2,1,0:T(8,128)(2,1)} %param.23) | copy-start | bytes 1769476
  6.5 59.7 %all-gather.2.cloned.1.call-start = ((), (), s32[]{:S(2)}) async-start(), calls=%async_computation.2 | async-start | bytes 1327104 | tf_op jit(solution)/shard_map/all_gather | solution.py:58
  18.9 17.9 %copy-start.8 = (s32[1,2]{1,0:T(1,128)S(1)}, s32[1,2]{1,0:T(1,128)}, u32[]{:S(2)}) copy-start(s32[1,2]{1,0:T(1,128)} %param.20) | copy-start | bytes 28
  19.4 17.5 %copy-start.4 = (bf16[2,16,2304]{2,1,0:T(8,128)(2,1)S(1)}, bf16[2,16,2304]{2,1,0:T(8,128)(2,1)}, u32[]{:S(2)}) copy-start(bf16[2,16,2304]{2,1,0:T(8,128)(2,1)} %param.16) | copy-start | bytes 442372
  20.2 1050.6 %all-reduce.3.cloned.1.call-start = ((), (), s32[]{:S(2)}) async-start(), calls=%async_computation.3 | async-start | bytes 4718592 | tf_op jit(solution)/shard_map/psum | solution.py:108
  69.6 494.6 %copy-start.1 = (bf16[1,2,64,2304]{2,3,1,0:T(8,128)(2,1)S(1)}, bf16[1,2,64,2304]{2,3,1,0:T(8,128)(2,1)}, u32[]{:S(2)}) copy-start(bf16[1,2,64,2304]{2,3,1,0:T(8,128)(2,1)} %copy.110) | copy-start | bytes 1769476
  574.7 0.8 copy-start.5
  574.7 652.8 %all-reduce.5.cloned.1.call-start = ((), (), s32[]{:S(2)}) async-start(), calls=%async_computation.4 | async-start | bytes 884736 | tf_op jit(solution)/shard_map/psum | solution.py:150
  1070.7 27.2 %copy-start.6 = (f32[2304]{0:T(1024)S(1)}, f32[2304]{0:T(1024)}, u32[]{:S(2)}) copy-start(f32[2304]{0:T(1024)} %param.24) | copy-start | bytes 27652
  1118.7 2.8 copy-start.2
  1121.3 115.0 %copy-start.7 = (bf16[2,16,2]{1,2,0:T(2,128)(2,1)S(1)}, bf16[2,16,2]{1,2,0:T(2,128)(2,1)}, u32[]{:S(2)}) copy-start(bf16[2,16,2]{1,2,0:T(2,128)(2,1)} %param.18) | copy-start | bytes 388
  1229.6 22.9 %all-to-all-start.1 = ((bf16[8,2,6,2304]{3,1,2,0:T(2,128)(2,1)}), bf16[8,2,6,2304]{3,1,2,0:T(2,128)(2,1)S(1)}, u32[]{:S(2)}, u32[]{:S(2)}) async-start(bf16[8,2,6,2304]{3,1,2,0:T(2,128)(2,1)} %copy.105), calls=%async_computation.1 | async-start | bytes 884736 | tf_op jit(solution)/shard_map/all_to_all | solution.py:151
Sparse Core Ops, SparseCore 0:
  20.3 45.9 all-gather.1
  574.8 197.8 all-reduce.2
  1122.6 104.7 all-reduce.4
where the time goes:
time: 1260 us
  blocking collectives  1060 us (84%)
  waiting for transfers between devices  131 us (10%)
  local copies, waits for them, and re-layouts  20.2 us (2%)
  between operations  13.4 us (1%)
  matrix products  12.9 us (1%)
    psum x1, blocking collectives, on_device(): context_all, totals_all = lax.psum((context, totals), ('exp', 'shard'))  491 us
    pmax x1, blocking collectives, on_device(): row_peak = lax.pmax(local_peak, ('exp', 'shard'))  490 us
    psum x1, waiting for transfers between devices, on_device(): expert_out = lax.psum(partial_out.astype(jnp.bfloat16), 'shard')  105 us
  transfers between devices with their start and end apart: 4, of which 3 were waited for; matrix products, arithmetic and copies ran while one was open for 1% of the time, Pallas kernels for 0%

commit v1 on v0

--- a/solution.py
+++ b/solution.py
@@ -147,7 +147,7 @@
         gate_up,
         down_proj,
     )
-    expert_out = lax.psum(partial_out.astype(jnp.bfloat16), "shard")
+    expert_out = jnp.sum(lax.all_gather(partial_out.astype(jnp.bfloat16), "shard"), axis=0)
     returned = lax.all_to_all(expert_out, "exp", split_axis=0, concat_axis=0, tiled=True)
     moe_term = jnp.einsum(
         "jtnc,njcd->jtd", share_table, returned, preferred_element_type=jnp.float32

time: 1260 us -> 1200 us (0.952)
  waiting for transfers between devices: 131 us -> 70 us
    psum x1 -> x0, waiting for transfers between devices: 105 us -> none  [on_device(): expert_out = lax.psum(partial_out.astype(jnp.bfloat16), 'shard')]
    all_gather x0 -> x1, waiting for transfers between devices: none -> 44.2 us  [on_device(): lax.all_gather(partial_out.astype(jnp.bfloat16), 'shard')]
where the time goes in v1:
time: 1200 us
  blocking collectives  1060 us (88%)
  waiting for transfers between devices  70 us (6%)
  local copies, waits for them, and re-layouts  18.9 us (2%)
  other arithmetic  15.8 us (1%)
  between operations  13.4 us (1%)
  matrix products  13.1 us (1%)
    psum x1, blocking collectives, on_device(): context_all, totals_all = lax.psum((context, totals), ('exp', 'shard'))  491 us
    pmax x1, blocking collectives, on_device(): row_peak = lax.pmax(local_peak, ('exp', 'shard'))  490 us
    all_gather x1, waiting for transfers between devices, on_device(): lax.all_gather(partial_out.astype(jnp.bfloat16), 'shard')  44.2 us
  transfers between devices with their start and end apart: 4, of which 3 were waited for; matrix products, arithmetic and copies ran while one was open for 1% of the time, Pallas kernels for 0%

profile of v1, /device:TPU:1, one launch (start us, length us, event | category | flops | bytes accessed | tf_op | source)
XLA Modules:
  0.0 1202.0 jit_solution(11537990163666701545)
XLA Ops:
  7.4 11.4 all_gather.25
  21.8 8.4 all_gather.28
  32.2 2.3 copy.111
  34.5 2.0 reshape_squeeze.6
  36.7 11.1 all_gather.24
  48.2 18.2 %all-gather.4.cloned.1.call-done = bf16[2,128,2304]{2,1,0:T(8,128)(2,1)} async-done(((bf16[2,16,2304]{2,1,0:T(8,128)(2,1)}), bf16[2,128,2304]{2,1,0:T(8,128)(2,1)}) %all-gather.4.cloned.1.call-update) | async-done | bytes 1179664 | tf_op jit(solution)/shard_map/all_gather | solution.py:58
  66.3 1.9 gather_fusion
  69.7 3.9 fusion.3
  73.6 490.0 %pmax.7 = f32[2,36,128]{2,1,0:T(8,128)S(1)} all-reduce(f32[2,36,128]{2,1,0:T(8,128)S(1)} %copy.93), channel_id=1, replica_groups=mesh['req'=4,'exp'=8,'shard'=16] {'exp','shard'}, use_global_device_ids=true, to_apply=%region_7.9 | all-reduce | flops 9216 | bytes 73728 | tf_op jit(solution)/shard_map/pmax | solution.py:96
  564.3 3.7 fusion.32
  567.9 3.1 copy.95
  571.0 3.7 select_reduce_fusion
  575.2 1.6 gather_fusion.4
  576.9 2.4 convert_reduce_fusion
  579.4 491.2 %psum.15 = f32[2,36,128]{2,0,1:T(2,128)S(1)} all-reduce(f32[2,36,128]{2,0,1:T(2,128)S(1)} %select_reduce_fusion.1), channel_id=1, replica_groups=mesh['req'=4,'exp'=8,'shard'=16] {'exp','shard'}, use_global_device_ids=true, to_apply=%region_12.14 | all-reduce | flops 9216 | bytes 73728 | tf_op jit(solution)/shard_map/psum | solution.py:108
  1071.2 1.5 convolution_convert_fusion.2
  1072.9 23.8 %all_gather.27 = bf16[2,16,2304]{1,0,2:T(2,128)(2,1)S(1)} all-gather(bf16[2,16,144]{1,0,2:T(2,128)(2,1)S(1)} %copy.97), channel_id=1, replica_groups=mesh['req'=4,'exp'=8,'shard'=16] {'shard'}, dimensions={2}, use_global_device_ids=true | all-gather | bytes 156672 | tf_op jit(solution)/shard_map/all_gather | solution.py:120
  1099.1 19.8 %all_to_all.10 = bf16[8,2,6,2304]{3,1,2,0:T(2,128)(2,1)S(1)} all-to-all(bf16[8,2,6,2304]{3,1,2,0:T(2,128)(2,1)S(1)} %copy.101), channel_id=1, replica_groups=mesh['req'=4,'exp'=8,'shard'=16] {'exp'}, dimensions={0} | all-to-all | bytes 884736 | tf_op jit(solution)/shard_map/all_to_all | solution.py:146
  1119.8 2.2 convolution_convert_fusion.1
  1122.1 44.2 %all-gather.6.cloned.1.call-done = bf16[128,2,6,2304]{3,0,2,1:T(8,128)(2,1)} async-done(((bf16[8,2,6,2304]{3,0,2,1:T(8,128)(2,1)}), bf16[128,2,6,2304]{3,0,2,1:T(8,128)(2,1)}) %all-gather.6.cloned.1.call-update) | async-done | bytes 7077904 | tf_op jit(solution)/shard_map/all_gather | solution.py:150
  1166.3 3.9 bitcast_reduce_fusion
  1171.3 7.1 all-to-all-start.1
  1178.4 7.9 all_gather.29
  1187.0 7.6 all-to-all-done.1
  (80 shorter events, 15.8 us)
Async XLA Ops:
  6.5 1112.5 %copy-start = (bf16[1,2,180,2304]{3,1,2,0:T(2,128)(2,1)S(1)}, bf16[1,2,180,2304]{3,1,2,0:T(2,128)(2,1)}, u32[]{:S(2)}) copy-start(bf16[1,2,180,2304]{3,1,2,0:T(2,128)(2,1)} %param.26) | copy-start | bytes 4976644
  6.5 28.0 %copy-start.2 = (bf16[1,2,64,2304]{3,2,1,0:T(8,128)(2,1)S(1)}, bf16[1,2,64,2304]{3,2,1,0:T(8,128)(2,1)}, u32[]{:S(2)}) copy-start(bf16[1,2,64,2304]{3,2,1,0:T(8,128)(2,1)} %param.22) | copy-start | bytes 1769476
  6.5 59.8 %all-gather.4.cloned.1.call-start = ((), (), s32[]{:S(2)}) async-start(), calls=%async_computation.2 | async-start | bytes 1327104 | tf_op jit(solution)/shard_map/all_gather | solution.py:58
  18.9 17.7 %copy-start.6 = (s32[1,2]{1,0:T(1,128)S(1)}, s32[1,2]{1,0:T(1,128)}, u32[]{:S(2)}) copy-start(s32[1,2]{1,0:T(1,128)} %param.20) | copy-start | bytes 28
  18.9 17.8 %copy-start.3 = (bf16[2,16,2304]{2,1,0:T(8,128)(2,1)S(1)}, bf16[2,16,2304]{2,1,0:T(8,128)(2,1)}, u32[]{:S(2)}) copy-start(bf16[2,16,2304]{2,1,0:T(8,128)(2,1)} %param.16) | copy-start | bytes 442372
  20.2 1051.0 %all-reduce.2.cloned.1.call-start = ((), (), s32[]{:S(2)}) async-start(), calls=%async_computation.3 | async-start | bytes 4718592 | tf_op jit(solution)/shard_map/psum | solution.py:108
  69.7 494.6 %copy-start.1 = (bf16[1,2,64,2304]{2,3,1,0:T(8,128)(2,1)S(1)}, bf16[1,2,64,2304]{2,3,1,0:T(8,128)(2,1)}, u32[]{:S(2)}) copy-start(bf16[1,2,64,2304]{2,3,1,0:T(8,128)(2,1)} %copy.111) | copy-start | bytes 1769476
  574.8 591.5 %all-gather.6.cloned.1.call-start = ((), (), s32[]{:S(2)}) async-start(), calls=%async_computation.4 | async-start | bytes 7520256 | tf_op jit(solution)/shard_map/all_gather | solution.py:150
  1071.2 27.2 %copy-start.4 = (f32[2304]{0:T(1024)S(1)}, f32[2304]{0:T(1024)}, u32[]{:S(2)}) copy-start(f32[2304]{0:T(1024)} %param.24) | copy-start | bytes 27652
  1122.1 56.3 %copy-start.5 = (bf16[2,16,2]{1,2,0:T(2,128)(2,1)S(1)}, bf16[2,16,2]{1,2,0:T(2,128)(2,1)}, u32[]{:S(2)}) copy-start(bf16[2,16,2]{1,2,0:T(2,128)(2,1)} %param.18) | copy-start | bytes 388
  1171.3 23.3 %all-to-all-start.1 = ((bf16[8,2,6,2304]{3,1,2,0:T(2,128)(2,1)}), bf16[8,2,6,2304]{3,1,2,0:T(2,128)(2,1)S(1)}, u32[]{:S(2)}, u32[]{:S(2)}) async-start(bf16[8,2,6,2304]{3,1,2,0:T(2,128)(2,1)} %copy.106), calls=%async_computation.1 | async-start | bytes 884736 | tf_op jit(solution)/shard_map/all_to_all | solution.py:151
Sparse Core Ops, SparseCore 0:
  20.3 45.9 all-gather.3
  574.9 197.8 all-reduce.1
  1122.2 44.0 all-gather.5
